TPU v7x, 32 devices: a whole 2x2x4 slice. The times are simulated.
32 devices in a mesh: freq: 4 (over x, core), tile: 8 (over z, y).
Axes of the slice: x: 2, y: 2, z: 4, core: 2. Of those that a mesh axis runs over, the one named last changes fastest.
Arguments:
- travel_time: float32 [512, 8, 512], P('tile', None, 'freq'), may hold values from 0 to 4
- crossing: int32 [8, 512], P('tile'), may hold values from 0 to 63
- bins: int32 [4], P('freq'), may hold values from 8 to 71
- transmission: float32 [4, 2, 64], P('freq'), may hold values from -1 to 1
- capture: bfloat16 [4, 2, 512, 512], P('freq', None, 'tile'), may hold values from -0.01171875 to 0.01171875
Outputs:
- image: float32 [2, 8, 512], P(None, 'tile')
All inputs are finite; a program needn't handle non-finite values.
Results may differ from a plain program's by a relative error of at most 0.0033.
Values may be sent and summed in bfloat16 or wider, within the bound.
No kernel may reach another device: no remote copies, remote signals or barrier semaphores. Data moves between devices by JAX's collectives and lax.ppermute only.
A program may use at most 64 MiB of HBM per device.

v0:
```python
import math
import jax
import jax.numpy as jnp
from jax import lax
from jax.sharding import PartitionSpec as P

TWO_PI = 2.0 * math.pi


def gather_shifted(block, axis_name, size):
    pieces = [block]
    for s in range(1, size):
        pairs = [(i, (i - s) % size) for i in range(size)]
        pieces.append(lax.ppermute(block, axis_name, pairs))
    return pieces


def chain(block, axis_name, size, stride, step, direction):
    positions = size // stride
    pairs = []
    for z in range(positions):
        target = z + direction
        if 0 <= target < positions and 0 <= z - direction * (step - 1) < positions:
            pairs += [(z * stride + y, target * stride + y) for y in range(stride)]
    return lax.ppermute(block, axis_name, pairs)


def line_gather(block, axis_name, size):
    positions = size // 2
    z = lax.axis_index(axis_name) // 2
    left = [block]
    right = [block]
    for j in range(1, positions):
        left.append(chain(left[-1], axis_name, size, 2, j, 1))
        right.append(chain(right[-1], axis_name, size, 2, j, -1))
    slots = left[:0:-1] + [block] + right[1:]
    return (slots, z)


def pair_swap(slots, axis_name, size):
    positions = size // 2
    centre = positions - 1
    out = []
    for i, piece in enumerate(slots):
        d = i - centre
        pairs = [
            (p * 2 + y, p * 2 + 1 - y)
            for p in range(positions)
            if 0 <= p + d < positions
            for y in range(2)
        ]
        out.append(lax.ppermute(piece, axis_name, pairs))
    return out


def gather_rows(block, axis_name, size):
    positions = size // 2
    slots, z = line_gather(block, axis_name, size)
    other = pair_swap(slots, axis_name, size)
    mine = lax.dynamic_slice_in_dim(jnp.stack(slots), positions - 1 - z, positions, 0)
    theirs = lax.dynamic_slice_in_dim(jnp.stack(other), positions - 1 - z, positions, 0)
    both = jnp.stack([mine, theirs], axis=1)
    both = jnp.roll(both, lax.axis_index(axis_name) % 2, axis=1)
    return both.reshape((size,) + block.shape)


def gather_columns(block, axis_name, size):
    outer = size // 2
    same_core = [block]
    for s in range(1, outer):
        pairs = [(i, (i - 2 * s) % size) for i in range(size)]
        same_core.append(lax.ppermute(block, axis_name, pairs))
    swap = [(i, i ^ 1) for i in range(size)]
    partner = [lax.ppermute(piece, axis_name, swap) for piece in same_core]
    return jnp.stack([jnp.stack(same_core), jnp.stack(partner)], axis=1)


def all_sum(value, axis_name, size):
    step = 1
    while step < size:
        pairs = [(i, i ^ step) for i in range(size)]
        value = value + lax.ppermute(value, axis_name, pairs)
        step *= 2
    return value


def body(travel_time, crossing, bins, transmission, capture):
    tiles = lax.axis_size("tile")
    freqs = lax.axis_size("freq")
    k = lax.axis_index("tile")
    f = lax.axis_index("freq")
    cap_all = gather_rows(capture[0], "tile", tiles)
    cap_all = jnp.moveaxis(cap_all, 0, 1)
    cap_real = cap_all[0].reshape(-1, cap_all.shape[-1])
    cap_imag = cap_all[1].reshape(-1, cap_all.shape[-1])
    rows = cap_real.shape[0]
    regrouped = lax.all_to_all(travel_time, "tile", split_axis=1, concat_axis=0, tiled=True)
    view = gather_columns(regrouped, "freq", freqs)
    view = jnp.moveaxis(view.reshape((freqs,) + regrouped.shape), 0, 2)
    elements, row_count, _, width = view.shape
    voxels = row_count * freqs * width
    scaled = TWO_PI * bins[0].astype(jnp.float32)
    angle = scaled * view.reshape(elements, voxels)
    field_real = jnp.cos(angle).astype(jnp.bfloat16)
    field_imag = (-jnp.sin(angle)).astype(jnp.bfloat16)
    stacked = jnp.concatenate([field_real, field_imag], axis=0)
    block = jnp.concatenate(
        [
            jnp.concatenate([cap_real, -cap_imag], axis=1),
            jnp.concatenate([cap_imag, cap_real], axis=1),
        ],
        axis=0,
    )
    product = jnp.dot(block, stacked, preferred_element_type=jnp.float32)
    w_real = product[:rows]
    w_imag = product[rows:]
    g_real = field_real.astype(jnp.float32)
    g_imag = field_imag.astype(jnp.float32)
    focus_real = jnp.sum(g_real * w_real - g_imag * w_imag, axis=0)
    focus_imag = jnp.sum(g_real * w_imag + g_imag * w_real, axis=0)
    outer = freqs // 2
    focus = jnp.stack([focus_real, focus_imag]).reshape(2, row_count, outer, 2, width)
    focus = jnp.roll(focus, f % 2, axis=3)
    focus = jnp.roll(focus, f // 2, axis=2).reshape(2, row_count, freqs * width)
    focus_real = focus[0]
    focus_imag = focus[1]
    cells = transmission.shape[2]
    match = crossing[None] == lax.broadcasted_iota(jnp.int32, (cells, 1, 1), 0)
    coeff_real = jnp.sum(
        jnp.where(match, transmission[0, 0][:, None, None], jnp.float32(0.0)), axis=0
    )
    coeff_imag = jnp.sum(
        jnp.where(match, transmission[0, 1][:, None, None], jnp.float32(0.0)), axis=0
    )
    square_real = coeff_real * coeff_real - coeff_imag * coeff_imag
    square_imag = 2.0 * coeff_real * coeff_imag
    part_real = square_real * focus_real - square_imag * focus_imag
    part_imag = square_real * focus_imag + square_imag * focus_real
    partial_image = jnp.stack([part_real, part_imag])
    return all_sum(partial_image, "freq", freqs)


def solution(mesh):
    in_specs = (
        P("tile", None, "freq"),
        P("tile", None),
        P("freq"),
        P("freq", None, None),
        P("freq", None, "tile", None),
    )
    out_specs = P(None, "tile", None)
    return jax.shard_map(body, mesh=mesh, in_specs=in_specs, out_specs=out_specs, check_vma=False)
```

profile of v0, /device:TPU:0, one launch (start us, length us, event | category | flops | bytes accessed | tf_op | source)
XLA Modules:
  0.0 63.5 jit_solution(8108796120977732849)
XLA Ops:
  0.0 5.1 %collective-permute-start.3 = (bf16[2,64,512]{2,1,0:T(8,128)(2,1)}, bf16[2,64,512]{2,1,0:T(8,128)(2,1)S(1)}, u32[]{:S(2)}, u32[]{:S(2)}) collective-permute-start(bf16[2,64,512]{2,1,0:T(8,128)(2,1)} %bitcast.102), channel_id=1, source_target_pairs={{0,2},{1,3},{2,4},{3,5},{4,6},{5,7},{8,10},{9,11},{10,12},{11,13},... | collective-permute-start | bytes 393224 | tf_op jit(solution)/shard_map/ppermute | solution.py:25
  5.1 1.6 %collective-permute-start.12 = (bf16[2,64,512]{2,1,0:T(8,128)(2,1)}, bf16[2,64,512]{2,1,0:T(8,128)(2,1)S(1)}, u32[]{:S(2)}, u32[]{:S(2)}) collective-permute-start(bf16[2,64,512]{2,1,0:T(8,128)(2,1)} %bitcast.103), channel_id=1, source_target_pairs={{0,1},{1,0},{2,3},{3,2},{4,5},{5,4},{6,7},{7,6},{8,9},{9,8},{10,11... | collective-permute-start | bytes 393224 | tf_op jit(solution)/shard_map/ppermute | solution.py:52
  6.7 1.3 %collective-permute-start.6 = (bf16[2,64,512]{2,1,0:T(8,128)(2,1)}, bf16[2,64,512]{2,1,0:T(8,128)(2,1)S(1)}, u32[]{:S(2)}, u32[]{:S(2)}) collective-permute-start(bf16[2,64,512]{2,1,0:T(8,128)(2,1)} %bitcast.104), channel_id=1, source_target_pairs={{2,0},{3,1},{4,2},{5,3},{6,4},{7,5},{10,8},{11,9},{12,10},{13,11},... | collective-permute-start | bytes 393224 | tf_op jit(solution)/shard_map/ppermute | solution.py:25
  7.9 1.7 %copy.14 = f32[64,8,128]{2,0,1:T(8,128)} copy(f32[64,8,128]{2,1,0:T(8,128)} %param.5) | data formatting | bytes 524288 | tf_op args[0]
  9.6 5.9 %all-to-all-start = ((f32[64,8,128]{2,0,1:T(8,128)}), f32[64,8,128]{2,0,1:T(8,128)S(1)}, u32[]{:S(2)}, u32[]{:S(2)}) async-start(f32[64,8,128]{2,0,1:T(8,128)} %copy.14), calls=%async_computation | async-start | bytes 524288 | tf_op jit(solution)/shard_map/all_to_all | solution.py:97
  15.6 0.7 %collective-permute-start.4 = (bf16[2,64,512]{2,1,0:T(8,128)(2,1)S(1)}, bf16[2,64,512]{2,1,0:T(8,128)(2,1)S(1)}, u32[]{:S(2)}, u32[]{:S(2)}) collective-permute-start(bf16[2,64,512]{2,1,0:T(8,128)(2,1)S(1)} %collective-permute-done.3), channel_id=1, source_target_pairs={{2,4},{3,5},{4,6},{5,7},{10,12},{11,13},{12,14},{13,15},{18,20},{1... | collective-permute-start | bytes 393224 | tf_op jit(solution)/shard_map/ppermute | solution.py:25
  16.3 0.8 %slice_bitcast_fusion = (f32[64]{0:T(128)S(1)}, f32[64]{0:T(128)S(1)}) fusion(f32[1,2,64]{2,1,0:T(2,128)} %param.8), kind=kLoop, calls=%fused_computation.67 | loop fusion | bytes 1024 | tf_op jit(solution)/shard_map/jit(_where)/broadcast_in_dim | solution.py:133
  17.7 0.8 %select_reduce_fusion.1 = (f32[512]{0:T(512)S(1)}, f32[512]{0:T(512)S(1)}) fusion(f32[64]{0:T(128)S(1)} %get-tuple-element.20, s32[512]{0:T(512)} %bitcast.111, f32[64]{0:T(128)S(1)} %get-tuple-element.19), kind=kLoop, calls=%fused_computation.49 | loop fusion | flops 162816 | bytes 6656 | tf_op jit(solution)/shard_map/reduce_sum | solution.py:129
  18.5 1.3 %collective-permute-start.7 = (bf16[2,64,512]{2,1,0:T(8,128)(2,1)S(1)}, bf16[2,64,512]{2,1,0:T(8,128)(2,1)S(1)}, u32[]{:S(2)}, u32[]{:S(2)}) collective-permute-start(bf16[2,64,512]{2,1,0:T(8,128)(2,1)S(1)} %collective-permute-done.6), channel_id=1, source_target_pairs={{2,0},{3,1},{4,2},{5,3},{10,8},{11,9},{12,10},{13,11},{18,16},{19,... | collective-permute-start | bytes 393224 | tf_op jit(solution)/shard_map/ppermute | solution.py:25
  19.8 0.7 %collective-permute-start.5 = (bf16[2,64,512]{2,1,0:T(8,128)(2,1)S(1)}, bf16[2,64,512]{2,1,0:T(8,128)(2,1)S(1)}, u32[]{:S(2)}, u32[]{:S(2)}) collective-permute-start(bf16[2,64,512]{2,1,0:T(8,128)(2,1)S(1)} %collective-permute-done.4), channel_id=1, source_target_pairs={{4,6},{5,7},{12,14},{13,15},{20,22},{21,23},{28,30},{29,31}} | collective-permute-start | bytes 393224 | tf_op jit(solution)/shard_map/ppermute | solution.py:25
  20.5 0.7 %collective-permute-start.11 = (bf16[2,64,512]{2,1,0:T(8,128)(2,1)S(1)}, bf16[2,64,512]{2,1,0:T(8,128)(2,1)S(1)}, u32[]{:S(2)}, u32[]{:S(2)}) collective-permute-start(bf16[2,64,512]{2,1,0:T(8,128)(2,1)S(1)} %collective-permute-done.3), channel_id=1, source_target_pairs={{2,3},{3,2},{4,5},{5,4},{6,7},{7,6},{10,11},{11,10},{12,13},{13,12... | collective-permute-start | bytes 393224 | tf_op jit(solution)/shard_map/ppermute | solution.py:52
  21.2 3.9 %collective-permute-start.13 = (bf16[2,64,512]{2,1,0:T(8,128)(2,1)S(1)}, bf16[2,64,512]{2,1,0:T(8,128)(2,1)S(1)}, u32[]{:S(2)}, u32[]{:S(2)}) collective-permute-start(bf16[2,64,512]{2,1,0:T(8,128)(2,1)S(1)} %collective-permute-done.6), channel_id=1, source_target_pairs={{0,1},{1,0},{2,3},{3,2},{4,5},{5,4},{8,9},{9,8},{10,11},{11,10},{1... | collective-permute-start | bytes 393224 | tf_op jit(solution)/shard_map/ppermute | solution.py:52
  25.1 3.0 %collective-permute-done.7 = bf16[2,64,512]{2,1,0:T(8,128)(2,1)S(1)} collective-permute-done((bf16[2,64,512]{2,1,0:T(8,128)(2,1)S(1)}, bf16[2,64,512]{2,1,0:T(8,128)(2,1)S(1)}, u32[]{:S(2)}, u32[]{:S(2)}) %collective-permute-start.7) | collective-permute-done | bytes 131104 | tf_op jit(solution)/shard_map/ppermute | solution.py:25
  28.1 0.7 %collective-permute-start.10 = (bf16[2,64,512]{2,1,0:T(8,128)(2,1)S(1)}, bf16[2,64,512]{2,1,0:T(8,128)(2,1)S(1)}, u32[]{:S(2)}, u32[]{:S(2)}) collective-permute-start(bf16[2,64,512]{2,1,0:T(8,128)(2,1)S(1)} %collective-permute-done.4), channel_id=1, source_target_pairs={{4,5},{5,4},{6,7},{7,6},{12,13},{13,12},{14,15},{15,14},{20,21},{2... | collective-permute-start | bytes 393224 | tf_op jit(solution)/shard_map/ppermute | solution.py:52
  28.7 1.3 %collective-permute-start.8 = (bf16[2,64,512]{2,1,0:T(8,128)(2,1)S(1)}, bf16[2,64,512]{2,1,0:T(8,128)(2,1)S(1)}, u32[]{:S(2)}, u32[]{:S(2)}) collective-permute-start(bf16[2,64,512]{2,1,0:T(8,128)(2,1)S(1)} %collective-permute-done.7), channel_id=1, source_target_pairs={{2,0},{3,1},{10,8},{11,9},{18,16},{19,17},{26,24},{27,25}} | collective-permute-start | bytes 393224 | tf_op jit(solution)/shard_map/ppermute | solution.py:25
  30.2 6.5 %collective-permute-done.8 = bf16[2,64,512]{2,1,0:T(8,128)(2,1)S(1)} collective-permute-done((bf16[2,64,512]{2,1,0:T(8,128)(2,1)S(1)}, bf16[2,64,512]{2,1,0:T(8,128)(2,1)S(1)}, u32[]{:S(2)}, u32[]{:S(2)}) %collective-permute-start.8) | collective-permute-done | bytes 131104 | tf_op jit(solution)/shard_map/ppermute | solution.py:25
  36.6 0.7 %collective-permute-start.9 = (bf16[2,64,512]{2,1,0:T(8,128)(2,1)S(1)}, bf16[2,64,512]{2,1,0:T(8,128)(2,1)S(1)}, u32[]{:S(2)}, u32[]{:S(2)}) collective-permute-start(bf16[2,64,512]{2,1,0:T(8,128)(2,1)S(1)} %collective-permute-done.5), channel_id=1, source_target_pairs={{6,7},{7,6},{14,15},{15,14},{22,23},{23,22},{30,31},{31,30}} | collective-permute-start | bytes 393224 | tf_op jit(solution)/shard_map/ppermute | solution.py:52
  37.4 3.4 %collective-permute-start.14 = (bf16[2,64,512]{2,1,0:T(8,128)(2,1)S(1)}, bf16[2,64,512]{2,1,0:T(8,128)(2,1)S(1)}, u32[]{:S(2)}, u32[]{:S(2)}) collective-permute-start(bf16[2,64,512]{2,1,0:T(8,128)(2,1)S(1)} %collective-permute-done.7), channel_id=1, source_target_pairs={{0,1},{1,0},{2,3},{3,2},{8,9},{9,8},{10,11},{11,10},{16,17},{17,16... | collective-permute-start | bytes 393224 | tf_op jit(solution)/shard_map/ppermute | solution.py:52
  40.8 2.5 %collective-permute-start.15 = (bf16[2,64,512]{2,1,0:T(8,128)(2,1)S(1)}, bf16[2,64,512]{2,1,0:T(8,128)(2,1)S(1)}, u32[]{:S(2)}, u32[]{:S(2)}) collective-permute-start(bf16[2,64,512]{2,1,0:T(8,128)(2,1)S(1)} %collective-permute-done.8), channel_id=1, source_target_pairs={{0,1},{1,0},{8,9},{9,8},{16,17},{17,16},{24,25},{25,24}} | collective-permute-start | bytes 393224 | tf_op jit(solution)/shard_map/ppermute | solution.py:52
  43.3 1.6 %collective-permute-start = (f32[512,1,128]{2,0,1:T(8,128)S(1)}, f32[512,1,128]{2,0,1:T(8,128)S(1)}, u32[]{:S(2)}, u32[]{:S(2)}) collective-permute-start(f32[512,1,128]{2,0,1:T(8,128)S(1)} %bitcast.95), channel_id=1, source_target_pairs={{0,16},{8,24},{16,0},{24,8},{1,17},{9,25},{17,1},{25,9},{2,18},{10... | collective-permute-start | bytes 786440 | tf_op jit(solution)/shard_map/ppermute | solution.py:72
  45.0 0.5 collective-permute-done.14
  45.5 2.2 %collective-permute-done.15 = bf16[2,64,512]{2,1,0:T(8,128)(2,1)S(1)} collective-permute-done((bf16[2,64,512]{2,1,0:T(8,128)(2,1)S(1)}, bf16[2,64,512]{2,1,0:T(8,128)(2,1)S(1)}, u32[]{:S(2)}, u32[]{:S(2)}) %collective-permute-start.15) | collective-permute-done | bytes 131104 | tf_op jit(solution)/shard_map/ppermute | solution.py:52
  47.7 0.7 %fusion.14 = bf16[4,2,2,64,512]{4,3,2,1,0:T(8,128)(2,1)S(1)} fusion(s32[]{:T(128)S(6)} %select_n.83, bf16[4,1,2,64,512]{4,3,2,1,0:T(8,128)(2,1)S(1)} %dynamic-slice_bitcast_fusion.1, bf16[4,1,2,64,512]{4,3,2,1,0:T(8,128)(2,1)S(1)} %dynamic-slice_bitcast_fusion), kind=kLoop, calls=%fused_computation.22 | loop fusion | flops 1572864 | bytes 2097156 | tf_op jit(solution)/shard_map/jit(_roll_dynamic)/concatenate | solution.py:63
  48.5 1.2 %collective-permute-done = f32[512,1,128]{2,0,1:T(8,128)S(1)} collective-permute-done((f32[512,1,128]{2,0,1:T(8,128)S(1)}, f32[512,1,128]{2,0,1:T(8,128)S(1)}, u32[]{:S(2)}, u32[]{:S(2)}) %collective-permute-start) | collective-permute-done | bytes 262176 | tf_op jit(solution)/shard_map/ppermute | solution.py:72
  49.9 1.4 %collective-permute-done.2 = f32[512,1,128]{2,0,1:T(8,128)S(1)} collective-permute-done((f32[512,1,128]{2,0,1:T(8,128)S(1)}, f32[512,1,128]{2,0,1:T(8,128)S(1)}, u32[]{:S(2)}, u32[]{:S(2)}) %collective-permute-start.2) | collective-permute-done | bytes 262176 | tf_op jit(solution)/shard_map/ppermute | solution.py:74
  51.3 3.8 %cosine_convert_fusion = (bf16[2,2,512,1,128]{4,2,0,3,1:T(8,128)(2,1)S(1)}, bf16[2,2,512,1,128]{4,2,0,3,1:T(8,128)(2,1)S(1)}) fusion(f32[2,1,512,1,128]{4,2,0,3,1:T(8,128)S(1)} %maximum_bitcast_fusion.1, f32[2,1,512,1,128]{4,2,0,3,1:T(8,128)S(1)} %maximum_bitcast_fusion, f32[]{:T(128)} %bitcast.4), kind=kLoop, calls=%fused_computation.28 | loop fusion | flops 1310720 | bytes 2097156 | tf_op jit(solution)/shard_map/convert.1
  56.2 1.2 %fusion = f32[1024,512]{1,0:T(8,128)S(1)} fusion(bf16[512,512]{1,0:T(8,128)(2,1)S(1)} %bitcast.98, bf16[512,512]{1,0:T(8,128)(2,1)S(1)} %bitcast.94, bf16[512,512]{1,0:T(8,128)(2,1)S(1)} %bitcast_negate_fusion, bf16[512,512]{1,0:T(8,128)(2,1)S(1)} %get-tuple-element.21, bf16[512,512]{1,0:T(8,128)(2,1)S(1)} %get-tuple-element.22), kind=kOutput, calls=%fused_computation.4 | convolution fusion | flops 1084227584 | bytes 4718592 | tf_op jit(solution)/shard_map/dot_general | solution.py:114
  57.5 0.4 fusion.11
  58.2 1.0 %collective-permute-done.16 = f32[2,1,512]{2,1,0:T(1,128)S(1)} collective-permute-done((f32[2,1,512]{2,1,0:T(1,128)S(1)}, f32[2,1,512]{2,1,0:T(1,128)S(1)}, u32[]{:S(2)}, u32[]{:S(2)}) %collective-permute-start.16) | collective-permute-done | bytes 4128 | tf_op jit(solution)/shard_map/ppermute | solution.py:82
  59.2 1.5 %collective-permute-start.17 = (f32[2,1,512]{2,1,0:T(1,128)S(1)}, f32[2,1,512]{2,1,0:T(1,128)S(1)}, u32[]{:S(2)}, u32[]{:S(2)}) collective-permute-start(f32[2,1,512]{2,1,0:T(1,128)S(1)} %fusion.23), channel_id=1, source_target_pairs={{0,16},{8,24},{16,0},{24,8},{1,17},{9,25},{17,1},{25,9},{2,18},{10... | collective-permute-start | bytes 12296 | tf_op jit(solution)/shard_map/ppermute | solution.py:82
  60.8 2.1 %collective-permute-done.17 = f32[2,1,512]{2,1,0:T(1,128)S(1)} collective-permute-done((f32[2,1,512]{2,1,0:T(1,128)S(1)}, f32[2,1,512]{2,1,0:T(1,128)S(1)}, u32[]{:S(2)}, u32[]{:S(2)}) %collective-permute-start.17) | collective-permute-done | bytes 4128 | tf_op jit(solution)/shard_map/ppermute | solution.py:82
  62.9 0.6 fusion.26
  (48 shorter events, 1.9 us)
Async XLA Ops:
  0.0 30.1 %copy-start = (bf16[1,2,64,512]{3,2,1,0:T(8,128)(2,1)S(1)}, bf16[1,2,64,512]{3,2,1,0:T(8,128)(2,1)}, u32[]{:S(2)}) copy-start(bf16[1,2,64,512]{3,2,1,0:T(8,128)(2,1)} %param.9) | copy-start | bytes 393220
  0.0 15.6 %collective-permute-start.3 = (bf16[2,64,512]{2,1,0:T(8,128)(2,1)}, bf16[2,64,512]{2,1,0:T(8,128)(2,1)S(1)}, u32[]{:S(2)}, u32[]{:S(2)}) collective-permute-start(bf16[2,64,512]{2,1,0:T(8,128)(2,1)} %bitcast.102), channel_id=1, source_target_pairs={{0,2},{1,3},{2,4},{3,5},{4,6},{5,7},{8,10},{9,11},{10,12},{11,13},... | collective-permute-start | bytes 393224 | tf_op jit(solution)/shard_map/ppermute | solution.py:25
  5.1 39.8 %collective-permute-start.12 = (bf16[2,64,512]{2,1,0:T(8,128)(2,1)}, bf16[2,64,512]{2,1,0:T(8,128)(2,1)S(1)}, u32[]{:S(2)}, u32[]{:S(2)}) collective-permute-start(bf16[2,64,512]{2,1,0:T(8,128)(2,1)} %bitcast.103), channel_id=1, source_target_pairs={{0,1},{1,0},{2,3},{3,2},{4,5},{5,4},{6,7},{7,6},{8,9},{9,8},{10,11... | collective-permute-start | bytes 393224 | tf_op jit(solution)/shard_map/ppermute | solution.py:52
  6.7 11.8 %collective-permute-start.6 = (bf16[2,64,512]{2,1,0:T(8,128)(2,1)}, bf16[2,64,512]{2,1,0:T(8,128)(2,1)S(1)}, u32[]{:S(2)}, u32[]{:S(2)}) collective-permute-start(bf16[2,64,512]{2,1,0:T(8,128)(2,1)} %bitcast.104), channel_id=1, source_target_pairs={{2,0},{3,1},{4,2},{5,3},{6,4},{7,5},{10,8},{11,9},{12,10},{13,11},... | collective-permute-start | bytes 393224 | tf_op jit(solution)/shard_map/ppermute | solution.py:25
  9.6 33.6 %all-to-all-start = ((f32[64,8,128]{2,0,1:T(8,128)}), f32[64,8,128]{2,0,1:T(8,128)S(1)}, u32[]{:S(2)}, u32[]{:S(2)}) async-start(f32[64,8,128]{2,0,1:T(8,128)} %copy.14), calls=%async_computation | async-start | bytes 524288 | tf_op jit(solution)/shard_map/all_to_all | solution.py:97
  15.6 4.2 %collective-permute-start.4 = (bf16[2,64,512]{2,1,0:T(8,128)(2,1)S(1)}, bf16[2,64,512]{2,1,0:T(8,128)(2,1)S(1)}, u32[]{:S(2)}, u32[]{:S(2)}) collective-permute-start(bf16[2,64,512]{2,1,0:T(8,128)(2,1)S(1)} %collective-permute-done.3), channel_id=1, source_target_pairs={{2,4},{3,5},{4,6},{5,7},{10,12},{11,13},{12,14},{13,15},{18,20},{1... | collective-permute-start | bytes 393224 | tf_op jit(solution)/shard_map/ppermute | solution.py:25
  18.5 9.6 %collective-permute-start.7 = (bf16[2,64,512]{2,1,0:T(8,128)(2,1)S(1)}, bf16[2,64,512]{2,1,0:T(8,128)(2,1)S(1)}, u32[]{:S(2)}, u32[]{:S(2)}) collective-permute-start(bf16[2,64,512]{2,1,0:T(8,128)(2,1)S(1)} %collective-permute-done.6), channel_id=1, source_target_pairs={{2,0},{3,1},{4,2},{5,3},{10,8},{11,9},{12,10},{13,11},{18,16},{19,... | collective-permute-start | bytes 393224 | tf_op jit(solution)/shard_map/ppermute | solution.py:25
  19.8 8.9 %collective-permute-start.5 = (bf16[2,64,512]{2,1,0:T(8,128)(2,1)S(1)}, bf16[2,64,512]{2,1,0:T(8,128)(2,1)S(1)}, u32[]{:S(2)}, u32[]{:S(2)}) collective-permute-start(bf16[2,64,512]{2,1,0:T(8,128)(2,1)S(1)} %collective-permute-done.4), channel_id=1, source_target_pairs={{4,6},{5,7},{12,14},{13,15},{20,22},{21,23},{28,30},{29,31}} | collective-permute-start | bytes 393224 | tf_op jit(solution)/shard_map/ppermute | solution.py:25
  20.5 22.8 %collective-permute-start.11 = (bf16[2,64,512]{2,1,0:T(8,128)(2,1)S(1)}, bf16[2,64,512]{2,1,0:T(8,128)(2,1)S(1)}, u32[]{:S(2)}, u32[]{:S(2)}) collective-permute-start(bf16[2,64,512]{2,1,0:T(8,128)(2,1)S(1)} %collective-permute-done.3), channel_id=1, source_target_pairs={{2,3},{3,2},{4,5},{5,4},{6,7},{7,6},{10,11},{11,10},{12,13},{13,12... | collective-permute-start | bytes 393224 | tf_op jit(solution)/shard_map/ppermute | solution.py:52
  21.2 23.8 %collective-permute-start.13 = (bf16[2,64,512]{2,1,0:T(8,128)(2,1)S(1)}, bf16[2,64,512]{2,1,0:T(8,128)(2,1)S(1)}, u32[]{:S(2)}, u32[]{:S(2)}) collective-permute-start(bf16[2,64,512]{2,1,0:T(8,128)(2,1)S(1)} %collective-permute-done.6), channel_id=1, source_target_pairs={{0,1},{1,0},{2,3},{3,2},{4,5},{5,4},{8,9},{9,8},{10,11},{11,10},{1... | collective-permute-start | bytes 393224 | tf_op jit(solution)/shard_map/ppermute | solution.py:52
  28.1 12.7 %collective-permute-start.10 = (bf16[2,64,512]{2,1,0:T(8,128)(2,1)S(1)}, bf16[2,64,512]{2,1,0:T(8,128)(2,1)S(1)}, u32[]{:S(2)}, u32[]{:S(2)}) collective-permute-start(bf16[2,64,512]{2,1,0:T(8,128)(2,1)S(1)} %collective-permute-done.4), channel_id=1, source_target_pairs={{4,5},{5,4},{6,7},{7,6},{12,13},{13,12},{14,15},{15,14},{20,21},{2... | collective-permute-start | bytes 393224 | tf_op jit(solution)/shard_map/ppermute | solution.py:52
  28.7 7.9 %collective-permute-start.8 = (bf16[2,64,512]{2,1,0:T(8,128)(2,1)S(1)}, bf16[2,64,512]{2,1,0:T(8,128)(2,1)S(1)}, u32[]{:S(2)}, u32[]{:S(2)}) collective-permute-start(bf16[2,64,512]{2,1,0:T(8,128)(2,1)S(1)} %collective-permute-done.7), channel_id=1, source_target_pairs={{2,0},{3,1},{10,8},{11,9},{18,16},{19,17},{26,24},{27,25}} | collective-permute-start | bytes 393224 | tf_op jit(solution)/shard_map/ppermute | solution.py:25
  36.6 0.7 %collective-permute-start.9 = (bf16[2,64,512]{2,1,0:T(8,128)(2,1)S(1)}, bf16[2,64,512]{2,1,0:T(8,128)(2,1)S(1)}, u32[]{:S(2)}, u32[]{:S(2)}) collective-permute-start(bf16[2,64,512]{2,1,0:T(8,128)(2,1)S(1)} %collective-permute-done.5), channel_id=1, source_target_pairs={{6,7},{7,6},{14,15},{15,14},{22,23},{23,22},{30,31},{31,30}} | collective-permute-start | bytes 393224 | tf_op jit(solution)/shard_map/ppermute | solution.py:52
  37.4 8.1 %collective-permute-start.14 = (bf16[2,64,512]{2,1,0:T(8,128)(2,1)S(1)}, bf16[2,64,512]{2,1,0:T(8,128)(2,1)S(1)}, u32[]{:S(2)}, u32[]{:S(2)}) collective-permute-start(bf16[2,64,512]{2,1,0:T(8,128)(2,1)S(1)} %collective-permute-done.7), channel_id=1, source_target_pairs={{0,1},{1,0},{2,3},{3,2},{8,9},{9,8},{10,11},{11,10},{16,17},{17,16... | collective-permute-start | bytes 393224 | tf_op jit(solution)/shard_map/ppermute | solution.py:52
  40.8 6.9 %collective-permute-start.15 = (bf16[2,64,512]{2,1,0:T(8,128)(2,1)S(1)}, bf16[2,64,512]{2,1,0:T(8,128)(2,1)S(1)}, u32[]{:S(2)}, u32[]{:S(2)}) collective-permute-start(bf16[2,64,512]{2,1,0:T(8,128)(2,1)S(1)} %collective-permute-done.8), channel_id=1, source_target_pairs={{0,1},{1,0},{8,9},{9,8},{16,17},{17,16},{24,25},{25,24}} | collective-permute-start | bytes 393224 | tf_op jit(solution)/shard_map/ppermute | solution.py:52
  43.3 6.4 %collective-permute-start = (f32[512,1,128]{2,0,1:T(8,128)S(1)}, f32[512,1,128]{2,0,1:T(8,128)S(1)}, u32[]{:S(2)}, u32[]{:S(2)}) collective-permute-start(f32[512,1,128]{2,0,1:T(8,128)S(1)} %bitcast.95), channel_id=1, source_target_pairs={{0,16},{8,24},{16,0},{24,8},{1,17},{9,25},{17,1},{25,9},{2,18},{10... | collective-permute-start | bytes 786440 | tf_op jit(solution)/shard_map/ppermute | solution.py:72
  44.9 5.0 %collective-permute-start.1 = (f32[512,1,128]{2,0,1:T(8,128)S(1)}, f32[512,1,128]{2,0,1:T(8,128)S(1)}, u32[]{:S(2)}, u32[]{:S(2)}) collective-permute-start(f32[512,1,128]{2,0,1:T(8,128)S(1)} %bitcast.96), channel_id=1, source_target_pairs={{0,8},{8,0},{16,24},{24,16},{1,9},{9,1},{17,25},{25,17},{2,10},{10... | collective-permute-start | bytes 786440 | tf_op jit(solution)/shard_map/ppermute | solution.py:74
  49.7 1.5 %collective-permute-start.2 = (f32[512,1,128]{2,0,1:T(8,128)S(1)}, f32[512,1,128]{2,0,1:T(8,128)S(1)}, u32[]{:S(2)}, u32[]{:S(2)}) collective-permute-start(f32[512,1,128]{2,0,1:T(8,128)S(1)} %collective-permute-done), channel_id=1, source_target_pairs={{0,8},{8,0},{16,24},{24,16},{1,9},{9,1},{17,25},{25,17},{2,10},{10... | collective-permute-start | bytes 786440 | tf_op jit(solution)/shard_map/ppermute | solution.py:74
  58.0 1.2 %collective-permute-start.16 = (f32[2,1,512]{2,1,0:T(1,128)S(1)}, f32[2,1,512]{2,1,0:T(1,128)S(1)}, u32[]{:S(2)}, u32[]{:S(2)}) collective-permute-start(f32[2,1,512]{2,1,0:T(1,128)S(1)} %pad_maximum_fusion), channel_id=1, source_target_pairs={{0,8},{8,0},{16,24},{24,16},{1,9},{9,1},{17,25},{25,17},{2,10},{10... | collective-permute-start | bytes 12296 | tf_op jit(solution)/shard_map/ppermute | solution.py:82
  59.2 3.7 %collective-permute-start.17 = (f32[2,1,512]{2,1,0:T(1,128)S(1)}, f32[2,1,512]{2,1,0:T(1,128)S(1)}, u32[]{:S(2)}, u32[]{:S(2)}) collective-permute-start(f32[2,1,512]{2,1,0:T(1,128)S(1)} %fusion.23), channel_id=1, source_target_pairs={{0,16},{8,24},{16,0},{24,8},{1,17},{9,25},{17,1},{25,9},{2,18},{10... | collective-permute-start | bytes 12296 | tf_op jit(solution)/shard_map/ppermute | solution.py:82
where the time goes:
time: 64 us; the launch traced here: 63.5 us
  starting transfers between devices  32.9 us (51%)
  waiting for transfers between devices  17.9 us (28%)
  other arithmetic  6.57 us (10%)
  local copies, waits for them, and re-layouts  3.82 us (6%)
  matrix products  1.24 us (2%)
  between operations  1.11 us (2%)
    ppermute x7, starting transfers between devices, pair_swap(): out.append(lax.ppermute(piece, axis_name, pairs))  13.3 us
    ppermute x6, starting transfers between devices, chain(): return lax.ppermute(block, axis_name, pairs)  10.3 us
    ppermute x6, waiting for transfers between devices, chain(): return lax.ppermute(block, axis_name, pairs)  9.43 us
    all_to_all x1, starting transfers between devices, body(): lax.all_to_all(travel_time, 'tile', split_axis=1, concat_axis=0, tiled=True)  5.94 us
    another operation x1, other arithmetic  3.84 us
    ppermute x2, waiting for transfers between devices, all_sum(): value = value + lax.ppermute(value, axis_name, pairs)  3.16 us
    ppermute x7, waiting for transfers between devices, pair_swap(): out.append(lax.ppermute(piece, axis_name, pairs))  2.63 us
    unnamed x15, local copies, waits for them, and re-layouts  1.84 us
  transfers between devices with their start and end apart: 19, of which 8 were waited for; matrix products, arithmetic and copies ran while one was open for 7% of the time, Pallas kernels for 0%

commit v1 on v0

--- a/solution.py
+++ b/solution.py
@@ -94,7 +94,12 @@
     cap_real = cap_all[0].reshape(-1, cap_all.shape[-1])
     cap_imag = cap_all[1].reshape(-1, cap_all.shape[-1])
     rows = cap_real.shape[0]
-    regrouped = lax.all_to_all(travel_time, "tile", split_axis=1, concat_axis=0, tiled=True)
+    regrouped = jnp.concatenate(
+        lax.all_to_all(
+            jnp.stack(jnp.split(travel_time, lax.axis_size("tile"), axis=1)), "tile", 0, 0
+        ),
+        axis=0,
+    )
     view = gather_columns(regrouped, "freq", freqs)
     view = jnp.moveaxis(view.reshape((freqs,) + regrouped.shape), 0, 2)
     elements, row_count, _, width = view.shape

time: 64 us -> 69.8 us (1.091)
  local copies, waits for them, and re-layouts: 3.82 us -> 9.57 us
    unnamed x15 -> x21, local copies, waits for them, and re-layouts: 1.84 us -> 4.37 us
    split x0 -> x1, local copies, waits for them, and re-layouts: none -> 2.42 us  [body(): jnp.split(travel_time, lax.axis_size('tile'), axis=1)]
    another operation x2 -> x3, local copies, waits for them, and re-layouts: 0.07 us -> 1.69 us
  transfers between devices with their start and end apart: 19 -> 19, of which waited for: 8 -> 8; matrix products, arithmetic and copies ran while one was open for 7% -> 14% of each run, Pallas kernels for 0% -> 0%
where the time goes in v1:
time: 69.8 us; the launch traced here: 69.2 us
  starting transfers between devices  32.9 us (47%)
  waiting for transfers between devices  17.8 us (26%)
  local copies, waits for them, and re-layouts  9.57 us (14%)
  other arithmetic  6.57 us (9%)
  matrix products  1.24 us (2%)
  between operations  1.11 us (2%)
    ppermute x7, starting transfers between devices, pair_swap(): out.append(lax.ppermute(piece, axis_name, pairs))  13.3 us
    ppermute x6, starting transfers between devices, chain(): return lax.ppermute(block, axis_name, pairs)  10.3 us
    ppermute x6, waiting for transfers between devices, chain(): return lax.ppermute(block, axis_name, pairs)  9.43 us
    all_to_all x1, starting transfers between devices, body(): lax.all_to_all(jnp.stack(jnp.split(travel_time, lax.axis_size('tile'), ax...  5.94 us
    unnamed x21, local copies, waits for them, and re-layouts  4.37 us
    another operation x1, other arithmetic  3.84 us
    ppermute x2, waiting for transfers between devices, all_sum(): value = value + lax.ppermute(value, axis_name, pairs)  3.14 us
    ppermute x7, waiting for transfers between devices, pair_swap(): out.append(lax.ppermute(piece, axis_name, pairs))  2.63 us
  transfers between devices with their start and end apart: 19, of which 8 were waited for; matrix products, arithmetic and copies ran while one was open for 14% of the time, Pallas kernels for 0%

profile of v1, /device:TPU:0, one launch (start us, length us, event | category | flops | bytes accessed | tf_op | source)
XLA Modules:
  0.0 69.2 jit_solution(4904044031238596953)
XLA Ops:
  0.0 5.1 %collective-permute-start.3 = (bf16[2,64,512]{2,1,0:T(8,128)(2,1)}, bf16[2,64,512]{2,1,0:T(8,128)(2,1)S(1)}, u32[]{:S(2)}, u32[]{:S(2)}) collective-permute-start(bf16[2,64,512]{2,1,0:T(8,128)(2,1)} %bitcast.127), channel_id=1, source_target_pairs={{0,2},{1,3},{2,4},{3,5},{4,6},{5,7},{8,10},{9,11},{10,12},{11,13},... | collective-permute-start | bytes 393224 | tf_op jit(solution)/shard_map/ppermute | solution.py:25
  5.1 1.6 %collective-permute-start.12 = (bf16[2,64,512]{2,1,0:T(8,128)(2,1)}, bf16[2,64,512]{2,1,0:T(8,128)(2,1)S(1)}, u32[]{:S(2)}, u32[]{:S(2)}) collective-permute-start(bf16[2,64,512]{2,1,0:T(8,128)(2,1)} %bitcast.128), channel_id=1, source_target_pairs={{0,1},{1,0},{2,3},{3,2},{4,5},{5,4},{6,7},{7,6},{8,9},{9,8},{10,11... | collective-permute-start | bytes 393224 | tf_op jit(solution)/shard_map/ppermute | solution.py:52
  6.7 1.3 %collective-permute-start.6 = (bf16[2,64,512]{2,1,0:T(8,128)(2,1)}, bf16[2,64,512]{2,1,0:T(8,128)(2,1)S(1)}, u32[]{:S(2)}, u32[]{:S(2)}) collective-permute-start(bf16[2,64,512]{2,1,0:T(8,128)(2,1)} %bitcast.129), channel_id=1, source_target_pairs={{2,0},{3,1},{4,2},{5,3},{6,4},{7,5},{10,8},{11,9},{12,10},{13,11},... | collective-permute-start | bytes 393224 | tf_op jit(solution)/shard_map/ppermute | solution.py:25
  7.9 2.4 %fusion.25 = (f32[64,1,128]{2,1,0:T(1,128)S(1)}, f32[64,1,128]{2,1,0:T(1,128)S(1)}, f32[64,1,128]{2,1,0:T(1,128)S(1)}, f32[64,1,128]{2,1,0:T(1,128)S(1)}, f32[64...) fusion(f32[64,8,128]{2,1,0:T(8,128)} %param.5), kind=kLoop, calls=%fused_computation.81 | loop fusion | bytes 524288 | tf_op jit(solution)/shard_map/split | solution.py:99
  10.4 0.6 constant_dynamic-update-slice_fusion.7
  11.0 0.6 constant_dynamic-update-slice_fusion.6
  14.6 0.6 constant_dynamic-update-slice_fusion
  15.2 5.9 %all-to-all-start = ((f32[8,64,1,128]{3,1,2,0:T(8,128)}), f32[8,64,1,128]{3,1,2,0:T(8,128)S(1)}, u32[]{:S(2)}, u32[]{:S(2)}) async-start(f32[8,64,1,128]{3,1,2,0:T(8,128)} %constant_dynamic-update-slice_fusion), calls=%async_computation | async-start | bytes 524288 | tf_op jit(solution)/shard_map/all_to_all | solution.py:98
  21.2 0.7 collective-permute-start.4
  21.8 0.8 %slice_bitcast_fusion = (f32[64]{0:T(128)S(1)}, f32[64]{0:T(128)S(1)}) fusion(f32[1,2,64]{2,1,0:T(2,128)} %param.8), kind=kLoop, calls=%fused_computation.75 | loop fusion | bytes 1024 | tf_op jit(solution)/shard_map/jit(_where)/broadcast_in_dim | solution.py:138
  23.3 0.8 %select_reduce_fusion.1 = (f32[512]{0:T(512)S(1)}, f32[512]{0:T(512)S(1)}) fusion(f32[64]{0:T(128)S(1)} %get-tuple-element.28, s32[512]{0:T(512)} %bitcast.136, f32[64]{0:T(128)S(1)} %get-tuple-element.27), kind=kLoop, calls=%fused_computation.49 | loop fusion | flops 162816 | bytes 6656 | tf_op jit(solution)/shard_map/reduce_sum | solution.py:134
  24.1 1.3 %collective-permute-start.7 = (bf16[2,64,512]{2,1,0:T(8,128)(2,1)S(1)}, bf16[2,64,512]{2,1,0:T(8,128)(2,1)S(1)}, u32[]{:S(2)}, u32[]{:S(2)}) collective-permute-start(bf16[2,64,512]{2,1,0:T(8,128)(2,1)S(1)} %collective-permute-done.6), channel_id=1, source_target_pairs={{2,0},{3,1},{4,2},{5,3},{10,8},{11,9},{12,10},{13,11},{18,16},{19,... | collective-permute-start | bytes 393224 | tf_op jit(solution)/shard_map/ppermute | solution.py:25
  25.4 0.7 collective-permute-start.5
  26.1 0.7 collective-permute-start.11
  26.8 3.9 %collective-permute-start.13 = (bf16[2,64,512]{2,1,0:T(8,128)(2,1)S(1)}, bf16[2,64,512]{2,1,0:T(8,128)(2,1)S(1)}, u32[]{:S(2)}, u32[]{:S(2)}) collective-permute-start(bf16[2,64,512]{2,1,0:T(8,128)(2,1)S(1)} %collective-permute-done.6), channel_id=1, source_target_pairs={{0,1},{1,0},{2,3},{3,2},{4,5},{5,4},{8,9},{9,8},{10,11},{11,10},{1... | collective-permute-start | bytes 393224 | tf_op jit(solution)/shard_map/ppermute | solution.py:52
  30.7 3.0 %collective-permute-done.7 = bf16[2,64,512]{2,1,0:T(8,128)(2,1)S(1)} collective-permute-done((bf16[2,64,512]{2,1,0:T(8,128)(2,1)S(1)}, bf16[2,64,512]{2,1,0:T(8,128)(2,1)S(1)}, u32[]{:S(2)}, u32[]{:S(2)}) %collective-permute-start.7) | collective-permute-done | bytes 131104 | tf_op jit(solution)/shard_map/ppermute | solution.py:25
  33.6 0.7 collective-permute-start.10
  34.3 1.3 %collective-permute-start.8 = (bf16[2,64,512]{2,1,0:T(8,128)(2,1)S(1)}, bf16[2,64,512]{2,1,0:T(8,128)(2,1)S(1)}, u32[]{:S(2)}, u32[]{:S(2)}) collective-permute-start(bf16[2,64,512]{2,1,0:T(8,128)(2,1)S(1)} %collective-permute-done.7), channel_id=1, source_target_pairs={{2,0},{3,1},{10,8},{11,9},{18,16},{19,17},{26,24},{27,25}} | collective-permute-start | bytes 393224 | tf_op jit(solution)/shard_map/ppermute | solution.py:25
  35.7 6.5 %collective-permute-done.8 = bf16[2,64,512]{2,1,0:T(8,128)(2,1)S(1)} collective-permute-done((bf16[2,64,512]{2,1,0:T(8,128)(2,1)S(1)}, bf16[2,64,512]{2,1,0:T(8,128)(2,1)S(1)}, u32[]{:S(2)}, u32[]{:S(2)}) %collective-permute-start.8) | collective-permute-done | bytes 131104 | tf_op jit(solution)/shard_map/ppermute | solution.py:25
  42.2 0.7 collective-permute-start.9
  42.9 3.4 %collective-permute-start.14 = (bf16[2,64,512]{2,1,0:T(8,128)(2,1)S(1)}, bf16[2,64,512]{2,1,0:T(8,128)(2,1)S(1)}, u32[]{:S(2)}, u32[]{:S(2)}) collective-permute-start(bf16[2,64,512]{2,1,0:T(8,128)(2,1)S(1)} %collective-permute-done.7), channel_id=1, source_target_pairs={{0,1},{1,0},{2,3},{3,2},{8,9},{9,8},{10,11},{11,10},{16,17},{17,16... | collective-permute-start | bytes 393224 | tf_op jit(solution)/shard_map/ppermute | solution.py:52
  46.4 2.5 %collective-permute-start.15 = (bf16[2,64,512]{2,1,0:T(8,128)(2,1)S(1)}, bf16[2,64,512]{2,1,0:T(8,128)(2,1)S(1)}, u32[]{:S(2)}, u32[]{:S(2)}) collective-permute-start(bf16[2,64,512]{2,1,0:T(8,128)(2,1)S(1)} %collective-permute-done.8), channel_id=1, source_target_pairs={{0,1},{1,0},{8,9},{9,8},{16,17},{17,16},{24,25},{25,24}} | collective-permute-start | bytes 393224 | tf_op jit(solution)/shard_map/ppermute | solution.py:52
  48.9 1.6 %collective-permute-start = (f32[512,1,128]{2,0,1:T(8,128)S(1)}, f32[512,1,128]{2,0,1:T(8,128)S(1)}, u32[]{:S(2)}, u32[]{:S(2)}) collective-permute-start(f32[512,1,128]{2,0,1:T(8,128)S(1)} %bitcast.112), channel_id=1, source_target_pairs={{0,16},{8,24},{16,0},{24,8},{1,17},{9,25},{17,1},{25,9},{2,18},{10... | collective-permute-start | bytes 786440 | tf_op jit(solution)/shard_map/ppermute | solution.py:72
  51.0 2.2 %collective-permute-done.15 = bf16[2,64,512]{2,1,0:T(8,128)(2,1)S(1)} collective-permute-done((bf16[2,64,512]{2,1,0:T(8,128)(2,1)S(1)}, bf16[2,64,512]{2,1,0:T(8,128)(2,1)S(1)}, u32[]{:S(2)}, u32[]{:S(2)}) %collective-permute-start.15) | collective-permute-done | bytes 131104 | tf_op jit(solution)/shard_map/ppermute | solution.py:52
  53.3 0.7 %fusion.14 = bf16[4,2,2,64,512]{4,3,2,1,0:T(8,128)(2,1)S(1)} fusion(s32[]{:T(128)S(6)} %select_n.83, bf16[4,1,2,64,512]{4,3,2,1,0:T(8,128)(2,1)S(1)} %dynamic-slice_bitcast_fusion.1, bf16[4,1,2,64,512]{4,3,2,1,0:T(8,128)(2,1)S(1)} %dynamic-slice_bitcast_fusion), kind=kLoop, calls=%fused_computation.22 | loop fusion | flops 1572864 | bytes 2097156 | tf_op jit(solution)/shard_map/jit(_roll_dynamic)/concatenate | solution.py:63
  54.1 1.2 %collective-permute-done = f32[512,1,128]{2,0,1:T(8,128)S(1)} collective-permute-done((f32[512,1,128]{2,0,1:T(8,128)S(1)}, f32[512,1,128]{2,0,1:T(8,128)S(1)}, u32[]{:S(2)}, u32[]{:S(2)}) %collective-permute-start) | collective-permute-done | bytes 262176 | tf_op jit(solution)/shard_map/ppermute | solution.py:72
  55.4 1.4 %collective-permute-done.2 = f32[512,1,128]{2,0,1:T(8,128)S(1)} collective-permute-done((f32[512,1,128]{2,0,1:T(8,128)S(1)}, f32[512,1,128]{2,0,1:T(8,128)S(1)}, u32[]{:S(2)}, u32[]{:S(2)}) %collective-permute-start.2) | collective-permute-done | bytes 262176 | tf_op jit(solution)/shard_map/ppermute | solution.py:74
  56.9 3.8 %cosine_convert_fusion = (bf16[2,2,512,1,128]{4,2,0,3,1:T(8,128)(2,1)S(1)}, bf16[2,2,512,1,128]{4,2,0,3,1:T(8,128)(2,1)S(1)}) fusion(f32[2,1,512,1,128]{4,2,0,3,1:T(8,128)S(1)} %maximum_bitcast_fusion.1, f32[2,1,512,1,128]{4,2,0,3,1:T(8,128)S(1)} %maximum_bitcast_fusion, f32[]{:T(128)} %bitcast.4), kind=kLoop, calls=%fused_computation.28 | loop fusion | flops 1310720 | bytes 2097156 | tf_op jit(solution)/shard_map/convert.1
  62.0 1.2 %fusion = f32[1024,512]{1,0:T(8,128)S(1)} fusion(bf16[512,512]{1,0:T(8,128)(2,1)S(1)} %bitcast.115, bf16[512,512]{1,0:T(8,128)(2,1)S(1)} %bitcast.111, bf16[512,512]{1,0:T(8,128)(2,1)S(1)} %bitcast_negate_fusion, bf16[512,512]{1,0:T(8,128)(2,1)S(1)} %get-tuple-element.29, bf16[512,512]{1,0:T(8,128)(2,1)S(1)} %get-tuple-element.30), kind=kOutput, calls=%fused_computation.4 | convolution fusion | flops 1084227584 | bytes 4718592 | tf_op jit(solution)/shard_map/dot_general | solution.py:119
  63.9 1.0 %collective-permute-done.16 = f32[2,1,512]{2,1,0:T(1,128)S(1)} collective-permute-done((f32[2,1,512]{2,1,0:T(1,128)S(1)}, f32[2,1,512]{2,1,0:T(1,128)S(1)}, u32[]{:S(2)}, u32[]{:S(2)}) %collective-permute-start.16) | collective-permute-done | bytes 4128 | tf_op jit(solution)/shard_map/ppermute | solution.py:82
  65.0 1.6 %collective-permute-start.17 = (f32[2,1,512]{2,1,0:T(1,128)S(1)}, f32[2,1,512]{2,1,0:T(1,128)S(1)}, u32[]{:S(2)}, u32[]{:S(2)}) collective-permute-start(f32[2,1,512]{2,1,0:T(1,128)S(1)} %fusion.23), channel_id=1, source_target_pairs={{0,16},{8,24},{16,0},{24,8},{1,17},{9,25},{17,1},{25,9},{2,18},{10... | collective-permute-start | bytes 12296 | tf_op jit(solution)/shard_map/ppermute | solution.py:82
  66.5 2.1 %collective-permute-done.17 = f32[2,1,512]{2,1,0:T(1,128)S(1)} collective-permute-done((f32[2,1,512]{2,1,0:T(1,128)S(1)}, f32[2,1,512]{2,1,0:T(1,128)S(1)}, u32[]{:S(2)}, u32[]{:S(2)}) %collective-permute-start.17) | collective-permute-done | bytes 4128 | tf_op jit(solution)/shard_map/ppermute | solution.py:82
  (54 shorter events, 6.5 us)
Async XLA Ops:
  0.0 35.7 %copy-start = (bf16[1,2,64,512]{3,2,1,0:T(8,128)(2,1)S(1)}, bf16[1,2,64,512]{3,2,1,0:T(8,128)(2,1)}, u32[]{:S(2)}) copy-start(bf16[1,2,64,512]{3,2,1,0:T(8,128)(2,1)} %param.9) | copy-start | bytes 393220
  0.0 21.2 %collective-permute-start.3 = (bf16[2,64,512]{2,1,0:T(8,128)(2,1)}, bf16[2,64,512]{2,1,0:T(8,128)(2,1)S(1)}, u32[]{:S(2)}, u32[]{:S(2)}) collective-permute-start(bf16[2,64,512]{2,1,0:T(8,128)(2,1)} %bitcast.127), channel_id=1, source_target_pairs={{0,2},{1,3},{2,4},{3,5},{4,6},{5,7},{8,10},{9,11},{10,12},{11,13},... | collective-permute-start | bytes 393224 | tf_op jit(solution)/shard_map/ppermute | solution.py:25
  5.1 45.4 %collective-permute-start.12 = (bf16[2,64,512]{2,1,0:T(8,128)(2,1)}, bf16[2,64,512]{2,1,0:T(8,128)(2,1)S(1)}, u32[]{:S(2)}, u32[]{:S(2)}) collective-permute-start(bf16[2,64,512]{2,1,0:T(8,128)(2,1)} %bitcast.128), channel_id=1, source_target_pairs={{0,1},{1,0},{2,3},{3,2},{4,5},{5,4},{6,7},{7,6},{8,9},{9,8},{10,11... | collective-permute-start | bytes 393224 | tf_op jit(solution)/shard_map/ppermute | solution.py:52
  6.7 17.4 %collective-permute-start.6 = (bf16[2,64,512]{2,1,0:T(8,128)(2,1)}, bf16[2,64,512]{2,1,0:T(8,128)(2,1)S(1)}, u32[]{:S(2)}, u32[]{:S(2)}) collective-permute-start(bf16[2,64,512]{2,1,0:T(8,128)(2,1)} %bitcast.129), channel_id=1, source_target_pairs={{2,0},{3,1},{4,2},{5,3},{6,4},{7,5},{10,8},{11,9},{12,10},{13,11},... | collective-permute-start | bytes 393224 | tf_op jit(solution)/shard_map/ppermute | solution.py:25
  15.2 33.6 %all-to-all-start = ((f32[8,64,1,128]{3,1,2,0:T(8,128)}), f32[8,64,1,128]{3,1,2,0:T(8,128)S(1)}, u32[]{:S(2)}, u32[]{:S(2)}) async-start(f32[8,64,1,128]{3,1,2,0:T(8,128)} %constant_dynamic-update-slice_fusion), calls=%async_computation | async-start | bytes 524288 | tf_op jit(solution)/shard_map/all_to_all | solution.py:98
  21.2 4.2 %collective-permute-start.4 = (bf16[2,64,512]{2,1,0:T(8,128)(2,1)S(1)}, bf16[2,64,512]{2,1,0:T(8,128)(2,1)S(1)}, u32[]{:S(2)}, u32[]{:S(2)}) collective-permute-start(bf16[2,64,512]{2,1,0:T(8,128)(2,1)S(1)} %collective-permute-done.3), channel_id=1, source_target_pairs={{2,4},{3,5},{4,6},{5,7},{10,12},{11,13},{12,14},{13,15},{18,20},{1... | collective-permute-start | bytes 393224 | tf_op jit(solution)/shard_map/ppermute | solution.py:25
  24.1 9.6 %collective-permute-start.7 = (bf16[2,64,512]{2,1,0:T(8,128)(2,1)S(1)}, bf16[2,64,512]{2,1,0:T(8,128)(2,1)S(1)}, u32[]{:S(2)}, u32[]{:S(2)}) collective-permute-start(bf16[2,64,512]{2,1,0:T(8,128)(2,1)S(1)} %collective-permute-done.6), channel_id=1, source_target_pairs={{2,0},{3,1},{4,2},{5,3},{10,8},{11,9},{12,10},{13,11},{18,16},{19,... | collective-permute-start | bytes 393224 | tf_op jit(solution)/shard_map/ppermute | solution.py:25
  25.4 8.9 %collective-permute-start.5 = (bf16[2,64,512]{2,1,0:T(8,128)(2,1)S(1)}, bf16[2,64,512]{2,1,0:T(8,128)(2,1)S(1)}, u32[]{:S(2)}, u32[]{:S(2)}) collective-permute-start(bf16[2,64,512]{2,1,0:T(8,128)(2,1)S(1)} %collective-permute-done.4), channel_id=1, source_target_pairs={{4,6},{5,7},{12,14},{13,15},{20,22},{21,23},{28,30},{29,31}} | collective-permute-start | bytes 393224 | tf_op jit(solution)/shard_map/ppermute | solution.py:25
  26.1 22.8 %collective-permute-start.11 = (bf16[2,64,512]{2,1,0:T(8,128)(2,1)S(1)}, bf16[2,64,512]{2,1,0:T(8,128)(2,1)S(1)}, u32[]{:S(2)}, u32[]{:S(2)}) collective-permute-start(bf16[2,64,512]{2,1,0:T(8,128)(2,1)S(1)} %collective-permute-done.3), channel_id=1, source_target_pairs={{2,3},{3,2},{4,5},{5,4},{6,7},{7,6},{10,11},{11,10},{12,13},{13,12... | collective-permute-start | bytes 393224 | tf_op jit(solution)/shard_map/ppermute | solution.py:52
  26.8 23.8 %collective-permute-start.13 = (bf16[2,64,512]{2,1,0:T(8,128)(2,1)S(1)}, bf16[2,64,512]{2,1,0:T(8,128)(2,1)S(1)}, u32[]{:S(2)}, u32[]{:S(2)}) collective-permute-start(bf16[2,64,512]{2,1,0:T(8,128)(2,1)S(1)} %collective-permute-done.6), channel_id=1, source_target_pairs={{0,1},{1,0},{2,3},{3,2},{4,5},{5,4},{8,9},{9,8},{10,11},{11,10},{1... | collective-permute-start | bytes 393224 | tf_op jit(solution)/shard_map/ppermute | solution.py:52
  33.6 12.7 %collective-permute-start.10 = (bf16[2,64,512]{2,1,0:T(8,128)(2,1)S(1)}, bf16[2,64,512]{2,1,0:T(8,128)(2,1)S(1)}, u32[]{:S(2)}, u32[]{:S(2)}) collective-permute-start(bf16[2,64,512]{2,1,0:T(8,128)(2,1)S(1)} %collective-permute-done.4), channel_id=1, source_target_pairs={{4,5},{5,4},{6,7},{7,6},{12,13},{13,12},{14,15},{15,14},{20,21},{2... | collective-permute-start | bytes 393224 | tf_op jit(solution)/shard_map/ppermute | solution.py:52
  34.3 7.9 %collective-permute-start.8 = (bf16[2,64,512]{2,1,0:T(8,128)(2,1)S(1)}, bf16[2,64,512]{2,1,0:T(8,128)(2,1)S(1)}, u32[]{:S(2)}, u32[]{:S(2)}) collective-permute-start(bf16[2,64,512]{2,1,0:T(8,128)(2,1)S(1)} %collective-permute-done.7), channel_id=1, source_target_pairs={{2,0},{3,1},{10,8},{11,9},{18,16},{19,17},{26,24},{27,25}} | collective-permute-start | bytes 393224 | tf_op jit(solution)/shard_map/ppermute | solution.py:25
  42.2 0.7 %collective-permute-start.9 = (bf16[2,64,512]{2,1,0:T(8,128)(2,1)S(1)}, bf16[2,64,512]{2,1,0:T(8,128)(2,1)S(1)}, u32[]{:S(2)}, u32[]{:S(2)}) collective-permute-start(bf16[2,64,512]{2,1,0:T(8,128)(2,1)S(1)} %collective-permute-done.5), channel_id=1, source_target_pairs={{6,7},{7,6},{14,15},{15,14},{22,23},{23,22},{30,31},{31,30}} | collective-permute-start | bytes 393224 | tf_op jit(solution)/shard_map/ppermute | solution.py:52
  42.9 8.1 %collective-permute-start.14 = (bf16[2,64,512]{2,1,0:T(8,128)(2,1)S(1)}, bf16[2,64,512]{2,1,0:T(8,128)(2,1)S(1)}, u32[]{:S(2)}, u32[]{:S(2)}) collective-permute-start(bf16[2,64,512]{2,1,0:T(8,128)(2,1)S(1)} %collective-permute-done.7), channel_id=1, source_target_pairs={{0,1},{1,0},{2,3},{3,2},{8,9},{9,8},{10,11},{11,10},{16,17},{17,16... | collective-permute-start | bytes 393224 | tf_op jit(solution)/shard_map/ppermute | solution.py:52
  46.4 6.9 %collective-permute-start.15 = (bf16[2,64,512]{2,1,0:T(8,128)(2,1)S(1)}, bf16[2,64,512]{2,1,0:T(8,128)(2,1)S(1)}, u32[]{:S(2)}, u32[]{:S(2)}) collective-permute-start(bf16[2,64,512]{2,1,0:T(8,128)(2,1)S(1)} %collective-permute-done.8), channel_id=1, source_target_pairs={{0,1},{1,0},{8,9},{9,8},{16,17},{17,16},{24,25},{25,24}} | collective-permute-start | bytes 393224 | tf_op jit(solution)/shard_map/ppermute | solution.py:52
  48.9 6.4 %collective-permute-start = (f32[512,1,128]{2,0,1:T(8,128)S(1)}, f32[512,1,128]{2,0,1:T(8,128)S(1)}, u32[]{:S(2)}, u32[]{:S(2)}) collective-permute-start(f32[512,1,128]{2,0,1:T(8,128)S(1)} %bitcast.112), channel_id=1, source_target_pairs={{0,16},{8,24},{16,0},{24,8},{1,17},{9,25},{17,1},{25,9},{2,18},{10... | collective-permute-start | bytes 786440 | tf_op jit(solution)/shard_map/ppermute | solution.py:72
  50.5 5.0 %collective-permute-start.1 = (f32[512,1,128]{2,0,1:T(8,128)S(1)}, f32[512,1,128]{2,0,1:T(8,128)S(1)}, u32[]{:S(2)}, u32[]{:S(2)}) collective-permute-start(f32[512,1,128]{2,0,1:T(8,128)S(1)} %bitcast.113), channel_id=1, source_target_pairs={{0,8},{8,0},{16,24},{24,16},{1,9},{9,1},{17,25},{25,17},{2,10},{10... | collective-permute-start | bytes 786440 | tf_op jit(solution)/shard_map/ppermute | solution.py:74
  55.3 1.5 %collective-permute-start.2 = (f32[512,1,128]{2,0,1:T(8,128)S(1)}, f32[512,1,128]{2,0,1:T(8,128)S(1)}, u32[]{:S(2)}, u32[]{:S(2)}) collective-permute-start(f32[512,1,128]{2,0,1:T(8,128)S(1)} %collective-permute-done), channel_id=1, source_target_pairs={{0,8},{8,0},{16,24},{24,16},{1,9},{9,1},{17,25},{25,17},{2,10},{10... | collective-permute-start | bytes 786440 | tf_op jit(solution)/shard_map/ppermute | solution.py:74
  63.7 1.2 %collective-permute-start.16 = (f32[2,1,512]{2,1,0:T(1,128)S(1)}, f32[2,1,512]{2,1,0:T(1,128)S(1)}, u32[]{:S(2)}, u32[]{:S(2)}) collective-permute-start(f32[2,1,512]{2,1,0:T(1,128)S(1)} %pad_maximum_fusion), channel_id=1, source_target_pairs={{0,8},{8,0},{16,24},{24,16},{1,9},{9,1},{17,25},{25,17},{2,10},{10... | collective-permute-start | bytes 12296 | tf_op jit(solution)/shard_map/ppermute | solution.py:82
  65.0 3.7 %collective-permute-start.17 = (f32[2,1,512]{2,1,0:T(1,128)S(1)}, f32[2,1,512]{2,1,0:T(1,128)S(1)}, u32[]{:S(2)}, u32[]{:S(2)}) collective-permute-start(f32[2,1,512]{2,1,0:T(1,128)S(1)} %fusion.23), channel_id=1, source_target_pairs={{0,16},{8,24},{16,0},{24,8},{1,17},{9,25},{17,1},{25,9},{2,18},{10... | collective-permute-start | bytes 12296 | tf_op jit(solution)/shard_map/ppermute | solution.py:82
